TPU v7x, 32 devices: a whole 2x2x4 slice. The times are simulated.
32 devices in a mesh: groups: 2 (over x), chan: 16 (over z, y, core), freq: 1.
Axes of the slice: x: 2, y: 2, z: 4, core: 2. Of those that a mesh axis runs over, the one named last changes fastest.
Arguments:
- raw: bfloat16 [256, 16, 12000], P(('groups', 'chan'), 'freq'), parts along dimension 0, may hold values from -100 to 100, as said below
- lengths: int32 [256, 16], P(('groups', 'chan'), 'freq'), parts along dimension 0, may hold values from 6000 to 12000
- quality: int32 [256], P('groups'), parts along dimension 0, may hold values 0 or 1
- assignment: int32 [256], P('groups'), parts along dimension 0, may hold values from 0 to 127, as said below
Outputs:
- cross: bfloat16 [512, 256, 2, 128], P('freq', ('groups', 'chan')), parts along dimension 1
There are 2 independent parts, one for each index of `groups`. A program takes and returns all parts, laid end to end along the dimension named above; each array names one. Nothing has to cross between parts.
Inputs may be any that keep to these rules, and one draw needn't show every extreme that they name: `raw`: records are clipped to this range. `assignment`: A permutation. The 8 channels of one file block (consecutive entries) land at most 1 in any one block of 8 consecutive positions, and some pair of blocks reaches 1.
All inputs are finite; a program needn't handle non-finite values.
Results may differ from a plain program's by a relative error of at most 0.012.
The roundings to bfloat16 on the way count: a program that leaves them out, or rounds other values in their place, can miss the bound.
Values may be sent and summed in bfloat16 or wider, within the bound.
No kernel may reach another device: no remote copies, remote signals or barrier semaphores. Data moves between devices by JAX's collectives and lax.ppermute only.
A program may use at most 128 MiB of HBM per device.

v0:
```python
import math
import jax
import jax.numpy as jnp
from jax import lax
from jax.sharding import PartitionSpec as P

WIN = 12000
NB = 512
K0 = 6
SUB = 32


def dft_table(first_sample, sample_count):
    samples = first_sample + jnp.arange(sample_count, dtype=jnp.int32)
    bin_index = K0 + jnp.arange(NB, dtype=jnp.int32)
    residue = samples[:, None] * bin_index[None, :] % WIN
    angles = residue.astype(jnp.float32) * (2.0 * math.pi / WIN)
    return jnp.concatenate([jnp.cos(angles), -jnp.sin(angles)], axis=1).astype(jnp.bfloat16)


def prepare(raw_block, valid_lengths):
    positions = jnp.arange(WIN, dtype=jnp.int32)
    inside = positions[None, None, :] < valid_lengths[:, :, None]
    values = raw_block.astype(jnp.float32)
    kept = jnp.where(inside, values, 0.0)
    average = jnp.sum(kept, axis=-1) / valid_lengths.astype(jnp.float32)
    taper = 0.5 - 0.5 * jnp.cos(positions.astype(jnp.float32) * (2.0 * math.pi / WIN))
    return jnp.where(inside, (values - average[:, :, None]) * taper[None, None, :], 0.0).astype(
        jnp.bfloat16
    )


def whiten(spectra):
    row_count = spectra.shape[0]
    grouped = spectra.reshape(row_count, 2, NB // SUB, SUB)
    power = jnp.sum(grouped * grouped, axis=(1, 3)) / SUB
    factor = lax.rsqrt(power + 1e-06)
    return (grouped * factor[:, None, :, None]).reshape(row_count, 2, NB).astype(jnp.bfloat16)


def spectra_of(shaped_rows):
    row_count = shaped_rows.shape[0]
    pieces = 8
    block_width = WIN // pieces
    total = jnp.zeros((row_count, 2 * NB), jnp.float32)
    for block_index in range(pieces):
        first_sample = block_index * block_width
        segment = lax.slice_in_dim(shaped_rows, first_sample, first_sample + block_width, axis=1)
        total = total + jnp.dot(
            segment, dft_table(first_sample, block_width), preferred_element_type=jnp.float32
        )
    return whiten(total)


def cross_block(left_rows, right_rows, all_windows):
    bins_here = left_rows.shape[3]
    left_side = left_rows.transpose(3, 0, 2, 1).reshape(
        bins_here, left_rows.shape[0], 2 * all_windows
    )
    right_count = right_rows.shape[0]
    right_plain = right_rows.transpose(3, 2, 1, 0).reshape(bins_here, 2 * all_windows, right_count)
    turned = jnp.stack([-right_rows[:, :, 1], right_rows[:, :, 0]], axis=2)
    right_turned = turned.transpose(3, 2, 1, 0).reshape(bins_here, 2 * all_windows, right_count)
    real_part = jnp.einsum(
        "bik,bkj->bij", left_side, right_plain, preferred_element_type=jnp.float32
    )
    imag_part = jnp.einsum(
        "bik,bkj->bij", left_side, right_turned, preferred_element_type=jnp.float32
    )
    return (jnp.stack([real_part, imag_part], axis=2) / all_windows).astype(jnp.bfloat16)


def body(raw, lengths, quality, assignment):
    channel_count = lax.axis_size("chan")
    my_index = lax.axis_index("chan")
    block_rows, window_count, sample_count = raw.shape
    capacity = max(1, block_rows // channel_count)
    total_channels = assignment.shape[0]
    targets_all = assignment.reshape(channel_count, block_rows) // block_rows
    row_numbers = jnp.arange(block_rows, dtype=jnp.int32)
    same_target = targets_all[:, :, None] == targets_all[:, None, :]
    earlier = row_numbers[None, None, :] < row_numbers[None, :, None]
    slot_table = jnp.sum(jnp.logical_and(same_target, earlier), axis=2)
    quality_table = quality.reshape(channel_count, block_rows)
    my_targets = lax.dynamic_index_in_dim(targets_all, my_index, 0, keepdims=False)
    my_slots = lax.dynamic_index_in_dim(slot_table, my_index, 0, keepdims=False)
    my_quality = lax.dynamic_index_in_dim(quality_table, my_index, 0, keepdims=False)
    device_numbers = jnp.arange(channel_count, dtype=jnp.int32)
    slot_numbers = jnp.arange(capacity, dtype=jnp.int32)
    match_table = jnp.logical_and(
        jnp.logical_and(
            my_targets[None, None, :] == device_numbers[:, None, None],
            my_slots[None, None, :] == slot_numbers[None, :, None],
        ),
        my_quality[None, None, :] == 1,
    )
    present = jnp.any(match_table, axis=2).reshape(-1)
    source_row = jnp.sum(jnp.where(match_table, row_numbers[None, None, :], 0), axis=2).reshape(-1)
    inverse = (
        jnp.zeros((total_channels,), jnp.int32)
        .at[assignment]
        .set(jnp.arange(total_channels, dtype=jnp.int32))
    )
    arrivals = lax.dynamic_slice_in_dim(inverse, my_index * block_rows, block_rows)
    source_device = arrivals // block_rows
    flat_slot = source_device * capacity + jnp.take(slot_table.reshape(-1), arrivals)
    arrival_good = jnp.take(quality, arrivals)
    shaped = prepare(raw, lengths)
    picked = jnp.take(shaped, source_row, axis=0)
    kept_rows = picked * present.astype(shaped.dtype).reshape((-1,) + (1,) * (shaped.ndim - 1))
    arrived = lax.all_to_all(
        kept_rows.reshape((channel_count, capacity) + shaped.shape[1:]),
        "chan",
        split_axis=0,
        concat_axis=0,
        tiled=True,
    )
    flat_rows = arrived.reshape((channel_count * capacity,) + arrived.shape[2:])
    picked = jnp.take(flat_rows, flat_slot, axis=0)
    local_rows = picked * arrival_good.astype(arrived.dtype).reshape(
        (-1,) + (1,) * (arrived.ndim - 2)
    )
    whitened = spectra_of(local_rows.reshape(block_rows * window_count, sample_count)).reshape(
        block_rows, window_count, 2, NB
    )
    panel = lax.all_to_all(whitened, "freq", split_axis=3, concat_axis=1, tiled=True)
    all_windows = panel.shape[1]
    return cross_block(panel, lax.all_gather(panel, "chan", axis=0, tiled=True), all_windows)


def solution(mesh):
    return jax.shard_map(
        body,
        mesh=mesh,
        in_specs=(
            P(("groups", "chan"), "freq", None),
            P(("groups", "chan"), "freq"),
            P("groups"),
            P("groups"),
        ),
        out_specs=P("freq", ("groups", "chan"), None, None),
        check_vma=False,
    )
```

profile of v0, /device:TPU:0, one launch (start us, length us, event | category | flops | bytes accessed | tf_op | source)
XLA Modules:
  0.0 277.0 jit_solution(14290823064365634316)
XLA Ops:
  6.5 0.7 reshape.391
  7.3 0.7 reshape.389
  8.1 0.1 convert_reduce_fusion
  8.2 0.2 fusion.113
  8.4 0.1 select_reduce_fusion
  8.5 0.1 fusion.114
  8.6 0.2 multiply_subtract_fusion
  8.8 3.3 %fusion = f32[8,16]{1,0:T(8,128)S(1)} fusion(bf16[8,16,12000]{2,1,0:T(8,128)(2,1)} %param.6, s32[8,16]{1,0:T(8,128)} %param.7), kind=kLoop, calls=%fused_computation.7 | loop fusion | flops 6143872 | bytes 3073024 | tf_op jit(solution)/shard_map/reduce_sum | solution.py:26
  12.1 1.5 fusion.3
  13.6 3.5 %gather_fusion = bf16[16,16,12000]{2,1,0:T(8,128)(2,1)} fusion(bf16[8,16,12000]{2,1,0:T(8,128)(2,1)S(1)} %fusion.3, s32[1024]{0:T(1024)S(1)} %pad_clamp_fusion.1), kind=kCustom, calls=%fused_computation.2 | custom fusion | bytes 12288064 | tf_op jit(solution)/shard_map/jit(_take)/gather | solution.py:109
  17.2 6.0 %fusion.4 = bf16[16,1,16,12000]{3,2,1,0:T(8,128)(2,1)} fusion(bf16[16,16,12000]{2,1,0:T(8,128)(2,1)} %gather_fusion, pred[16]{0:T(512)(128)(4,1)S(1)} %compare_and_fusion.1, bf16[16]{0:T(256)(128)(2,1)S(1)} %convert_element_type.89), kind=kLoop, calls=%fused_computation.12 | loop fusion | flops 6144000 | bytes 12288048 | tf_op jit(solution)/shard_map/mul | solution.py:110
  23.1 7.6 %all-to-all-start = ((bf16[16,1,16,12000]{3,2,1,0:T(8,128)(2,1)}), bf16[16,1,16,12000]{3,2,1,0:T(8,128)(2,1)}, u32[]{:S(2)}, u32[]{:S(2)}) async-start(bf16[16,1,16,12000]{3,2,1,0:T(8,128)(2,1)} %fusion.4), calls=%async_computation | async-start | bytes 12320768 | tf_op jit(solution)/shard_map/all_to_all | solution.py:111
  30.9 1.2 scatter_custom_fusion
  32.0 0.1 compare_select_fusion.4
  32.1 0.6 gather_fusion.3
  32.8 0.1 select_convert_fusion
  32.9 0.1 mul.277
  33.0 0.1 reshape.390
  33.1 0.6 gather_fusion.2
  33.8 0.1 compare_and_fusion.2
  33.9 0.1 broadcast_in_dim.48
  34.1 109.5 %cosine_convert_fusion = (bf16[1500,512]{1,0:T(8,128)(2,1)}, bf16[1500,512]{1,0:T(8,128)(2,1)}, bf16[1500,512]{1,0:T(8,128)(2,1)}, bf16[1500,512]{1,0:T(8,128)(2...) fusion(s32[1500]{0:T(1024)S(1)} %get-tuple-element.40, ...), kind=kLoop, calls=%fused_computation.76 | loop fusion | flops 73728000 | bytes 24620048 | tf_op jit(solution)/shard_map/convert
  143.6 3.5 %gather_fusion.1 = bf16[8,16,12000]{2,1,0:T(8,128)(2,1)S(1)} fusion(bf16[16,16,12000]{2,1,0:T(8,128)(2,1)} %bitcast.5, s32[1024]{0:T(1024)S(1)} %pad_clamp_fusion), kind=kCustom, calls=%fused_computation.3 | custom fusion | bytes 6144032 | tf_op jit(solution)/shard_map/jit(_take)/gather | solution.py:119
  147.1 0.5 fusion.54
  147.6 0.9 copy-done.17
  148.5 0.5 copy-done.18
  149.0 0.6 fusion.22
  149.5 0.8 copy-done.15
  150.4 0.5 copy-done.16
  150.8 0.6 fusion.97
  151.5 0.8 copy-done.13
  152.2 0.5 copy-done.14
  152.7 0.6 fusion.94
  153.3 0.8 copy-done.11
  154.1 0.5 copy-done.12
  154.5 0.6 fusion.91
  155.2 0.8 copy-done.9
  155.9 0.5 copy-done.10
  156.4 0.6 fusion.88
  157.0 0.8 copy-done.7
  157.8 0.5 copy-done.8
  158.3 0.6 fusion.85
  158.9 0.8 copy-done.5
  159.7 0.5 copy-done.6
  160.1 0.6 fusion.82
  160.8 0.8 copy-done.3
  161.5 0.5 copy-done.4
  162.0 0.6 fusion.127
  162.6 0.2 copy.38
  162.9 0.1 copy.39
  163.0 0.4 reshape.393
  163.4 0.3 mul.307
  163.8 0.4 mul.308
  164.2 0.8 fusion.100
  165.0 1.7 copy.42
  166.8 70.6 %all-gather.2.cloned.1.call-done = bf16[128,16,2,512]{3,1,2,0:T(8,128)(2,1)} async-done(((bf16[8,16,2,512]{3,1,2,0:T(8,128)(2,1)}), bf16[128,16,2,512]{3,1,2,0:T(8,128)(2,1)}) %all-gather.2.cloned.1.call-update) | async-done | bytes 4194320 | tf_op jit(solution)/shard_map/all_gather | solution.py:128
  237.4 9.1 %copy.41 = bf16[512,2,16,128]{3,2,1,0:T(8,128)(2,1)} copy(bf16[512,2,16,128]{0,2,1,3:T(8,128)(2,1)} %bitcast.37) | data formatting | bytes 8388608 | tf_op jit(solution)/shard_map/transpose | solution.py:61
  246.5 2.5 slice_negate_fusion
  249.0 2.3 maximum_bitcast_fusion
  251.3 9.1 %copy.43 = bf16[512,2,16,128]{3,2,1,0:T(8,128)(2,1)} copy(bf16[512,2,16,128]{0,2,1,3:T(8,128)(2,1)} %maximum_bitcast_fusion) | data formatting | bytes 8388608 | tf_op jit(solution)/shard_map/transpose | solution.py:63
  260.5 3.5 %convolution_bitcast_fusion.1 = f32[512,8,1,128]{3,1,0,2:T(8,128)S(1)} fusion(bf16[512,8,32]{2,1,0:T(8,128)(2,1)S(1)} %copy.42, bf16[512,32,128]{2,1,0:T(8,128)(2,1)} %bitcast.35), kind=kOutput, calls=%fused_computation.125 | convolution fusion | flops 33554432 | bytes 6553600 | tf_op jit(solution)/shard_map/bik,bkj->bij/dot_general | solution.py:64
  264.0 1.3 convolution_bitcast_fusion
  265.3 0.4 fusion.5
  265.6 4.6 %copy.45 = bf16[512,8,2,128]{3,2,1,0:T(2,128)(2,1)} copy(bf16[512,8,2,128]{3,1,0,2:T(8,128)(2,1)S(1)} %fusion.5) | data formatting | bytes 4194304 | tf_op jit(solution)/shard_map/convert_element_type | solution.py:70
  (53 shorter events, 0.6 us)
Async XLA Ops:
  6.5 5.5 %copy-start.19 = (s32[8,16]{1,0:T(8,128)S(1)}, s32[8,16]{1,0:T(8,128)}, u32[]{:S(2)}) copy-start(s32[8,16]{1,0:T(8,128)} %param.7) | copy-start | bytes 1540
  8.1 4.0 %copy-start.2 = (bf16[8,16,12000]{2,1,0:T(8,128)(2,1)S(1)}, bf16[8,16,12000]{2,1,0:T(8,128)(2,1)}, u32[]{:S(2)}) copy-start(bf16[8,16,12000]{2,1,0:T(8,128)(2,1)} %param.6) | copy-start | bytes 9216004
  23.1 7.7 %copy-start.20 = (s32[128]{0:T(128)S(1)}, s32[128]{0:T(128)}, u32[]{:S(2)}) copy-start(s32[128]{0:T(128)} %param.9) | copy-start | bytes 1540
  23.1 9.0 %copy-start = (s32[128]{0:T(128)S(1)}, s32[128]{0:T(128)}, u32[]{:S(2)}) copy-start(s32[128]{0:T(128)} %param.8) | copy-start | bytes 1540
  23.1 120.5 %all-to-all-start = ((bf16[16,1,16,12000]{3,2,1,0:T(8,128)(2,1)}), bf16[16,1,16,12000]{3,2,1,0:T(8,128)(2,1)}, u32[]{:S(2)}, u32[]{:S(2)}) async-start(bf16[16,1,16,12000]{3,2,1,0:T(8,128)(2,1)} %fusion.4), calls=%async_computation | async-start | bytes 12320768 | tf_op jit(solution)/shard_map/all_to_all | solution.py:111
  30.7 206.6 %all-gather.2.cloned.1.call-start = ((), (), s32[]{:S(2)}) async-start(), calls=%async_computation.1 | async-start | bytes 4456448 | tf_op jit(solution)/shard_map/all_gather | solution.py:128
  147.1 1.4 copy-start.17
  147.1 1.9 copy-start.18
  149.0 1.4 copy-start.15
  149.0 1.9 copy-start.16
  150.8 1.4 copy-start.13
  150.8 1.9 copy-start.14
  152.7 1.4 copy-start.11
  152.7 1.9 copy-start.12
  154.5 1.4 copy-start.9
  154.5 1.9 copy-start.10
  156.4 1.4 copy-start.7
  156.4 1.9 copy-start.8
  158.3 1.4 copy-start.5
  158.3 1.9 copy-start.6
  160.1 1.4 copy-start.3
  160.1 1.9 copy-start.4
  260.5 3.5 %copy-start.1 = (bf16[512,2,16,128]{3,2,1,0:T(8,128)(2,1)S(1)}, bf16[512,2,16,128]{3,2,1,0:T(8,128)(2,1)}, u32[]{:S(2)}) copy-start(bf16[512,2,16,128]{3,2,1,0:T(8,128)(2,1)} %copy.43) | copy-start | bytes 12582916
Sparse Core Ops, SparseCore 0:
  165.1 72.1 all-gather.1
where the time goes:
time: 278 us; the launch traced here: 277 us
  other arithmetic  128 us (46%)
  waiting for transfers between devices  70.6 us (25%)
  local copies, waits for them, and re-layouts  47.6 us (17%)
  between operations  13.7 us (5%)
  matrix products  9.73 us (4%)
  starting transfers between devices  7.63 us (3%)
    another operation x1, other arithmetic  110 us
    all_gather x1, waiting for transfers between devices, body(): lax.all_gather(panel, 'chan', axis=0, tiled=True)  70.6 us
    unnamed x42, local copies, waits for them, and re-layouts  10 us
    transpose x1, local copies, waits for them, and re-layouts, cross_block(): turned.transpose(3, 2, 1, 0)  9.15 us
    transpose x1, local copies, waits for them, and re-layouts, cross_block(): right_rows.transpose(3, 2, 1, 0)  9.12 us
    all_to_all x1, starting transfers between devices, body(): lax.all_to_all(kept_rows.reshape((channel_count, capacity) + shaped.shape...  7.59 us
    mul x1, other arithmetic, body(): picked * present.astype(shaped.dtype).reshape((-1,) + (1,) * (shaped.ndim...  5.97 us
  transfers between devices with their start and end apart: 2, of which 1 were waited for; matrix products, arithmetic and copies ran while one was open for 41% of the time, Pallas kernels for 0%

commit v1 on v0

--- a/solution.py
+++ b/solution.py
@@ -108,13 +108,19 @@
     shaped = prepare(raw, lengths)
     picked = jnp.take(shaped, source_row, axis=0)
     kept_rows = picked * present.astype(shaped.dtype).reshape((-1,) + (1,) * (shaped.ndim - 1))
-    arrived = lax.all_to_all(
-        kept_rows.reshape((channel_count, capacity) + shaped.shape[1:]),
-        "chan",
-        split_axis=0,
-        concat_axis=0,
-        tiled=True,
-    )
+    shard = kept_rows.reshape((channel_count, capacity) + shaped.shape[1:])
+    ways, here = (lax.axis_size("chan"), lax.axis_index("chan"))
+    width = shard.shape[0] // ways
+    shape = list(shard.shape)
+    shape[0] = width
+    height = shape[0]
+    shape[0] = height * ways
+    arrived = jnp.zeros(shape, shard.dtype)
+    for mask in range(ways):
+        part = lax.dynamic_slice_in_dim(shard, (here ^ mask) * width, width, axis=0)
+        if mask:
+            part = lax.ppermute(part, "chan", [(d, d ^ mask) for d in range(ways)])
+        arrived = lax.dynamic_update_slice_in_dim(arrived, part, (here ^ mask) * height, axis=0)
     flat_rows = arrived.reshape((channel_count * capacity,) + arrived.shape[2:])
     picked = jnp.take(flat_rows, flat_slot, axis=0)
     local_rows = picked * arrival_good.astype(arrived.dtype).reshape(

time: 278 us -> 412 us (1.48)
  waiting for transfers between devices: 70.6 us -> 180 us
  local copies, waits for them, and re-layouts: 47.6 us -> 64.4 us
  starting transfers between devices: 7.63 us -> 16.8 us
    ppermute x0 -> x15, waiting for transfers between devices: none -> 133 us  [body(): part = lax.ppermute(part, 'chan', [(d, d ^ mask) for d in range(ways)])]
    all_gather x1, waiting for transfers between devices: 70.6 us -> 47.2 us  [body(): lax.all_gather(panel, 'chan', axis=0, tiled=True)]
    ppermute x0 -> x15, starting transfers between devices: none -> 16.8 us  [body(): part = lax.ppermute(part, 'chan', [(d, d ^ mask) for d in range(ways)])]
    dynamic_update_slice x0 -> x15, local copies, waits for them, and re-layouts: none -> 11.7 us  [body(): lax.dynamic_update_slice_in_dim(arrived, part, (here ^ mask) * height, ax...]
    all_to_all x1 -> x0, starting transfers between devices: 7.59 us -> none  [body(): lax.all_to_all(kept_rows.reshape((channel_count, capacity) + shaped.shape...]
    unnamed x42 -> x54, local copies, waits for them, and re-layouts: 10 us -> 12.6 us
  transfers between devices with their start and end apart: 2 -> 16, of which waited for: 1 -> 11; matrix products, arithmetic and copies ran while one was open for 41% -> 30% of each run, Pallas kernels for 0% -> 0%
where the time goes in v1:
time: 412 us; the launch traced here: 411 us
  waiting for transfers between devices  180 us (44%)
  other arithmetic  127 us (31%)
  local copies, waits for them, and re-layouts  64.4 us (16%)
  starting transfers between devices  16.8 us (4%)
  between operations  13.9 us (3%)
  matrix products  9.73 us (2%)
    ppermute x15, waiting for transfers between devices, body(): part = lax.ppermute(part, 'chan', [(d, d ^ mask) for d in range(ways)])  133 us
    another operation x1, other arithmetic  109 us
    all_gather x1, waiting for transfers between devices, body(): lax.all_gather(panel, 'chan', axis=0, tiled=True)  47.2 us
    ppermute x15, starting transfers between devices, body(): part = lax.ppermute(part, 'chan', [(d, d ^ mask) for d in range(ways)])  16.8 us
    unnamed x54, local copies, waits for them, and re-layouts  12.6 us
    dynamic_update_slice x15, local copies, waits for them, and re-layouts, body(): lax.dynamic_update_slice_in_dim(arrived, part, (here ^ mask) * height, ax...  11.7 us
    transpose x1, local copies, waits for them, and re-layouts, cross_block(): turned.transpose(3, 2, 1, 0)  9.14 us
    transpose x1, local copies, waits for them, and re-layouts, cross_block(): right_rows.transpose(3, 2, 1, 0)  9.14 us
  transfers between devices with their start and end apart: 16, of which 11 were waited for; matrix products, arithmetic and copies ran while one was open for 30% of the time, Pallas kernels for 0%

profile of v1, /device:TPU:0, one launch (start us, length us, event | category | flops | bytes accessed | tf_op | source)
XLA Modules:
  0.0 411.3 jit_solution(5913103284761975053)
XLA Ops:
  6.5 0.7 reshape.463
  7.3 0.7 reshape.460
  8.8 3.0 fusion
  12.0 3.3 fusion.3
  15.3 3.6 gather_fusion
  18.9 3.4 select_multiply_fusion
  22.7 2.0 dynamic-slice_bitcast_fusion
  24.7 2.6 copy-done.2
  27.3 5.5 %collective-permute-start.14 = (bf16[1,1,16,12000]{3,2,1,0:T(8,128)(2,1)S(1)}, bf16[1,1,16,12000]{3,2,1,0:T(8,128)(2,1)S(1)}, u32[]{:S(2)}, u32[]{:S(2)}) collective-permute-start(bf16[1,1,16,12000]{3,2,1,0:T(8,128)(2,1)S(1)} %get-tuple-element.8), channel_id=1, source_target_pairs={{0,15},{1,14},{2,13},{3,12},{4,11},{5,10},{6,9},{7,8},{8,7},{9,6},... | collective-permute-start | bytes 1152008 | tf_op jit(solution)/shard_map/ppermute | solution.py:122
  33.4 3.2 collective-permute-start.12
  37.1 1.2 scatter_custom_fusion
  38.3 0.6 gather_fusion.3
  39.0 109.5 %cosine_convert_fusion = (bf16[1500,512]{1,0:T(8,128)(2,1)}, bf16[1500,512]{1,0:T(8,128)(2,1)}, bf16[1500,512]{1,0:T(8,128)(2,1)}, bf16[1500,512]{1,0:T(8,128)(2...) fusion(s32[1500]{0:T(1024)S(1)} %get-tuple-element.56, ...), kind=kLoop, calls=%fused_computation.75 | loop fusion | flops 73728000 | bytes 24620048 | tf_op jit(solution)/shard_map/convert
  148.9 0.6 gather_fusion.2
  149.9 1.4 collective-permute-start.1
  151.2 0.8 bitcast_dynamic-update-slice_fusion.14
  152.0 9.4 %collective-permute-done.1 = bf16[1,1,16,12000]{3,2,1,0:T(8,128)(2,1)S(1)} collective-permute-done((bf16[1,1,16,12000]{3,2,1,0:T(8,128)(2,1)}, bf16[1,1,16,12000]{3,2,1,0:T(8,128)(2,1)S(1)}, u32[]{:S(2)}, u32[]{:S(2)}) %collective-permute-start.1) | collective-permute-done | bytes 384032 | tf_op jit(solution)/shard_map/ppermute | solution.py:122
  161.4 0.7 collective-permute-start.2
  162.0 0.8 bitcast_dynamic-update-slice_fusion.13
  162.8 10.0 %collective-permute-done.2 = bf16[1,1,16,12000]{3,2,1,0:T(8,128)(2,1)S(1)} collective-permute-done((bf16[1,1,16,12000]{3,2,1,0:T(8,128)(2,1)}, bf16[1,1,16,12000]{3,2,1,0:T(8,128)(2,1)S(1)}, u32[]{:S(2)}, u32[]{:S(2)}) %collective-permute-start.2) | collective-permute-done | bytes 384032 | tf_op jit(solution)/shard_map/ppermute | solution.py:122
  172.8 0.8 bitcast_dynamic-update-slice_fusion.12
  173.6 10.3 %collective-permute-done.3 = bf16[1,1,16,12000]{3,2,1,0:T(8,128)(2,1)S(1)} collective-permute-done((bf16[1,1,16,12000]{3,2,1,0:T(8,128)(2,1)}, bf16[1,1,16,12000]{3,2,1,0:T(8,128)(2,1)S(1)}, u32[]{:S(2)}, u32[]{:S(2)}) %collective-permute-start.3) | collective-permute-done | bytes 384032 | tf_op jit(solution)/shard_map/ppermute | solution.py:122
  183.9 0.8 bitcast_dynamic-update-slice_fusion.11
  184.7 10.0 %collective-permute-done.4 = bf16[1,1,16,12000]{3,2,1,0:T(8,128)(2,1)S(1)} collective-permute-done((bf16[1,1,16,12000]{3,2,1,0:T(8,128)(2,1)}, bf16[1,1,16,12000]{3,2,1,0:T(8,128)(2,1)S(1)}, u32[]{:S(2)}, u32[]{:S(2)}) %collective-permute-start.4) | collective-permute-done | bytes 384032 | tf_op jit(solution)/shard_map/ppermute | solution.py:122
  194.7 1.2 collective-permute-start.5
  195.9 0.8 bitcast_dynamic-update-slice_fusion.10
  196.7 9.3 %collective-permute-done.5 = bf16[1,1,16,12000]{3,2,1,0:T(8,128)(2,1)S(1)} collective-permute-done((bf16[1,1,16,12000]{3,2,1,0:T(8,128)(2,1)S(1)}, bf16[1,1,16,12000]{3,2,1,0:T(8,128)(2,1)S(1)}, u32[]{:S(2)}, u32[]{:S(2)}) %collective-permute-start.5) | collective-permute-done | bytes 384032 | tf_op jit(solution)/shard_map/ppermute | solution.py:122
  206.0 0.7 collective-permute-start.6
  206.6 0.8 bitcast_dynamic-update-slice_fusion.9
  207.4 10.1 %collective-permute-done.6 = bf16[1,1,16,12000]{3,2,1,0:T(8,128)(2,1)S(1)} collective-permute-done((bf16[1,1,16,12000]{3,2,1,0:T(8,128)(2,1)S(1)}, bf16[1,1,16,12000]{3,2,1,0:T(8,128)(2,1)S(1)}, u32[]{:S(2)}, u32[]{:S(2)}) %collective-permute-start.6) | collective-permute-done | bytes 384032 | tf_op jit(solution)/shard_map/ppermute | solution.py:122
  217.6 3.3 collective-permute-start.7
  220.8 0.8 bitcast_dynamic-update-slice_fusion.8
  221.6 16.1 %collective-permute-done.7 = bf16[1,1,16,12000]{3,2,1,0:T(8,128)(2,1)S(1)} collective-permute-done((bf16[1,1,16,12000]{3,2,1,0:T(8,128)(2,1)S(1)}, bf16[1,1,16,12000]{3,2,1,0:T(8,128)(2,1)S(1)}, u32[]{:S(2)}, u32[]{:S(2)}) %collective-permute-start.7) | collective-permute-done | bytes 384032 | tf_op jit(solution)/shard_map/ppermute | solution.py:122
  237.7 0.8 bitcast_dynamic-update-slice_fusion.7
  238.5 19.2 %collective-permute-done.8 = bf16[1,1,16,12000]{3,2,1,0:T(8,128)(2,1)S(1)} collective-permute-done((bf16[1,1,16,12000]{3,2,1,0:T(8,128)(2,1)S(1)}, bf16[1,1,16,12000]{3,2,1,0:T(8,128)(2,1)S(1)}, u32[]{:S(2)}, u32[]{:S(2)}) %collective-permute-start.8) | collective-permute-done | bytes 384032 | tf_op jit(solution)/shard_map/ppermute | solution.py:122
  257.7 0.8 bitcast_dynamic-update-slice_fusion.6
  258.5 18.4 %collective-permute-done.9 = bf16[1,1,16,12000]{3,2,1,0:T(8,128)(2,1)S(1)} collective-permute-done((bf16[1,1,16,12000]{3,2,1,0:T(8,128)(2,1)S(1)}, bf16[1,1,16,12000]{3,2,1,0:T(8,128)(2,1)S(1)}, u32[]{:S(2)}, u32[]{:S(2)}) %collective-permute-start.9) | collective-permute-done | bytes 384032 | tf_op jit(solution)/shard_map/ppermute | solution.py:122
  276.9 0.8 bitcast_dynamic-update-slice_fusion.5
  277.7 19.6 %collective-permute-done.10 = bf16[1,1,16,12000]{3,2,1,0:T(8,128)(2,1)S(1)} collective-permute-done((bf16[1,1,16,12000]{3,2,1,0:T(8,128)(2,1)S(1)}, bf16[1,1,16,12000]{3,2,1,0:T(8,128)(2,1)S(1)}, u32[]{:S(2)}, u32[]{:S(2)}) %collective-permute-start.10) | collective-permute-done | bytes 384032 | tf_op jit(solution)/shard_map/ppermute | solution.py:122
  297.3 0.8 bitcast_dynamic-update-slice_fusion.4
  298.1 0.8 bitcast_dynamic-update-slice_fusion.3
  298.9 0.8 bitcast_dynamic-update-slice_fusion.2
  299.7 0.8 bitcast_dynamic-update-slice_fusion.1
  300.4 0.8 bitcast_dynamic-update-slice_fusion
  301.2 3.5 gather_fusion.1
  305.2 0.9 copy-done.17
  307.2 0.8 copy-done.15
  308.4 0.6 fusion.96
  309.1 0.8 copy-done.13
  310.9 0.8 copy-done.11
  312.8 0.8 copy-done.9
  314.7 0.8 copy-done.7
  316.5 0.8 copy-done.5
  318.4 0.8 copy-done.3
  321.8 0.8 fusion.99
  322.6 1.7 copy.42
  324.4 47.2 %all-gather.2.cloned.1.call-done = bf16[128,16,2,512]{3,1,2,0:T(8,128)(2,1)} async-done(((bf16[8,16,2,512]{3,1,2,0:T(8,128)(2,1)}), bf16[128,16,2,512]{3,1,2,0:T(8,128)(2,1)}) %all-gather.2.cloned.1.call-update) | async-done | bytes 4194320 | tf_op jit(solution)/shard_map/all_gather | solution.py:134
  371.6 9.1 %copy.41 = bf16[512,2,16,128]{3,2,1,0:T(8,128)(2,1)} copy(bf16[512,2,16,128]{0,2,1,3:T(8,128)(2,1)} %bitcast.92) | data formatting | bytes 8388608 | tf_op jit(solution)/shard_map/transpose | solution.py:61
  380.7 2.5 slice_negate_fusion
  383.2 2.4 maximum_bitcast_fusion
  385.6 9.1 %copy.43 = bf16[512,2,16,128]{3,2,1,0:T(8,128)(2,1)} copy(bf16[512,2,16,128]{0,2,1,3:T(8,128)(2,1)} %maximum_bitcast_fusion) | data formatting | bytes 8388608 | tf_op jit(solution)/shard_map/transpose | solution.py:63
  394.7 3.5 convolution_bitcast_fusion.1
  398.3 1.3 convolution_bitcast_fusion
  399.9 4.6 %copy.45 = bf16[512,8,2,128]{3,2,1,0:T(2,128)(2,1)} copy(bf16[512,8,2,128]{3,1,0,2:T(8,128)(2,1)S(1)} %fusion.4) | data formatting | bytes 4194304 | tf_op jit(solution)/shard_map/convert_element_type | solution.py:70
  (110 shorter events, 13.5 us)
Async XLA Ops:
  6.5 5.3 %copy-start.25 = (s32[8,16]{1,0:T(8,128)S(1)}, s32[8,16]{1,0:T(8,128)}, u32[]{:S(2)}) copy-start(s32[8,16]{1,0:T(8,128)} %param.7) | copy-start | bytes 1540
  6.5 365.0 %all-gather.2.cloned.1.call-start = ((), (), s32[]{:S(2)}) async-start(), calls=%async_computation | async-start | bytes 4456448 | tf_op jit(solution)/shard_map/all_gather | solution.py:134
  22.6 14.4 %copy-start.26 = (s32[128]{0:T(128)S(1)}, s32[128]{0:T(128)}, u32[]{:S(2)}) copy-start(s32[128]{0:T(128)} %param.9) | copy-start | bytes 1540
  22.6 15.7 %copy-start = (s32[128]{0:T(128)S(1)}, s32[128]{0:T(128)}, u32[]{:S(2)}) copy-start(s32[128]{0:T(128)} %param.8) | copy-start | bytes 1540
  24.7 2.6 copy-start.2
  27.3 273.1 %collective-permute-start.14 = (bf16[1,1,16,12000]{3,2,1,0:T(8,128)(2,1)S(1)}, bf16[1,1,16,12000]{3,2,1,0:T(8,128)(2,1)S(1)}, u32[]{:S(2)}, u32[]{:S(2)}) collective-permute-start(bf16[1,1,16,12000]{3,2,1,0:T(8,128)(2,1)S(1)} %get-tuple-element.8), channel_id=1, source_target_pairs={{0,15},{1,14},{2,13},{3,12},{4,11},{5,10},{6,9},{7,8},{8,7},{9,6},... | collective-permute-start | bytes 1152008 | tf_op jit(solution)/shard_map/ppermute | solution.py:122
  32.8 266.9 %collective-permute-start.13 = (bf16[1,1,16,12000]{3,2,1,0:T(8,128)(2,1)S(1)}, bf16[1,1,16,12000]{3,2,1,0:T(8,128)(2,1)S(1)}, u32[]{:S(2)}, u32[]{:S(2)}) collective-permute-start(bf16[1,1,16,12000]{3,2,1,0:T(8,128)(2,1)S(1)} %get-tuple-element.9), channel_id=1, source_target_pairs={{0,14},{1,15},{2,12},{3,13},{4,10},{5,11},{6,8},{7,9},{8,6},{9,7},... | collective-permute-start | bytes 1152008 | tf_op jit(solution)/shard_map/ppermute | solution.py:122
  33.4 265.5 %collective-permute-start.12 = (bf16[1,1,16,12000]{3,2,1,0:T(8,128)(2,1)S(1)}, bf16[1,1,16,12000]{3,2,1,0:T(8,128)(2,1)S(1)}, u32[]{:S(2)}, u32[]{:S(2)}) collective-permute-start(bf16[1,1,16,12000]{3,2,1,0:T(8,128)(2,1)S(1)} %get-tuple-element.10), channel_id=1, source_target_pairs={{0,13},{1,12},{2,15},{3,14},{4,9},{5,8},{6,11},{7,10},{8,5},{9,4},... | collective-permute-start | bytes 1152008 | tf_op jit(solution)/shard_map/ppermute | solution.py:122
  36.6 261.5 %collective-permute-start.11 = (bf16[1,1,16,12000]{3,2,1,0:T(8,128)(2,1)S(1)}, bf16[1,1,16,12000]{3,2,1,0:T(8,128)(2,1)S(1)}, u32[]{:S(2)}, u32[]{:S(2)}) collective-permute-start(bf16[1,1,16,12000]{3,2,1,0:T(8,128)(2,1)S(1)} %get-tuple-element.11), channel_id=1, source_target_pairs={{0,12},{1,13},{2,14},{3,15},{4,8},{5,9},{6,10},{7,11},{8,4},{9,5},... | collective-permute-start | bytes 1152008 | tf_op jit(solution)/shard_map/ppermute | solution.py:122
  36.9 112.9 %collective-permute-start = (bf16[1,1,16,12000]{3,2,1,0:T(8,128)(2,1)}, bf16[1,1,16,12000]{3,2,1,0:T(8,128)(2,1)S(1)}, u32[]{:S(2)}, u32[]{:S(2)}) collective-permute-start(bf16[1,1,16,12000]{3,2,1,0:T(8,128)(2,1)} %get-tuple-element.22), channel_id=1, source_target_pairs={{0,1},{1,0},{2,3},{3,2},{4,5},{5,4},{6,7},{7,6},{8,9},{9,8},{10,11... | collective-permute-start | bytes 1152008 | tf_op jit(solution)/shard_map/ppermute | solution.py:122
  149.8 44.9 %copy-start.24 = (bf16[1,1,16,12000]{3,2,1,0:T(8,128)(2,1)S(1)}, bf16[1,1,16,12000]{3,2,1,0:T(8,128)(2,1)}, u32[]{:S(2)}) copy-start(bf16[1,1,16,12000]{3,2,1,0:T(8,128)(2,1)} %get-tuple-element.17) | copy-start | bytes 1152004
  149.8 56.2 %copy-start.23 = (bf16[1,1,16,12000]{3,2,1,0:T(8,128)(2,1)S(1)}, bf16[1,1,16,12000]{3,2,1,0:T(8,128)(2,1)}, u32[]{:S(2)}) copy-start(bf16[1,1,16,12000]{3,2,1,0:T(8,128)(2,1)} %get-tuple-element.16) | copy-start | bytes 1152004
  149.8 67.8 %copy-start.22 = (bf16[1,1,16,12000]{3,2,1,0:T(8,128)(2,1)S(1)}, bf16[1,1,16,12000]{3,2,1,0:T(8,128)(2,1)}, u32[]{:S(2)}) copy-start(bf16[1,1,16,12000]{3,2,1,0:T(8,128)(2,1)} %get-tuple-element.15) | copy-start | bytes 1152004
  149.8 87.9 %copy-start.21 = (bf16[1,1,16,12000]{3,2,1,0:T(8,128)(2,1)S(1)}, bf16[1,1,16,12000]{3,2,1,0:T(8,128)(2,1)}, u32[]{:S(2)}) copy-start(bf16[1,1,16,12000]{3,2,1,0:T(8,128)(2,1)} %get-tuple-element.14) | copy-start | bytes 1152004
  149.9 11.5 %collective-permute-start.1 = (bf16[1,1,16,12000]{3,2,1,0:T(8,128)(2,1)}, bf16[1,1,16,12000]{3,2,1,0:T(8,128)(2,1)S(1)}, u32[]{:S(2)}, u32[]{:S(2)}) collective-permute-start(bf16[1,1,16,12000]{3,2,1,0:T(8,128)(2,1)} %get-tuple-element.21), channel_id=1, source_target_pairs={{0,2},{1,3},{2,0},{3,1},{4,6},{5,7},{6,4},{7,5},{8,10},{9,11},{10,... | collective-permute-start | bytes 1152008 | tf_op jit(solution)/shard_map/ppermute | solution.py:122
  151.2 106.5 %copy-start.20 = (bf16[1,1,16,12000]{3,2,1,0:T(8,128)(2,1)S(1)}, bf16[1,1,16,12000]{3,2,1,0:T(8,128)(2,1)}, u32[]{:S(2)}) copy-start(bf16[1,1,16,12000]{3,2,1,0:T(8,128)(2,1)} %get-tuple-element.13) | copy-start | bytes 1152004
  161.4 115.6 %copy-start.19 = (bf16[1,1,16,12000]{3,2,1,0:T(8,128)(2,1)S(1)}, bf16[1,1,16,12000]{3,2,1,0:T(8,128)(2,1)}, u32[]{:S(2)}) copy-start(bf16[1,1,16,12000]{3,2,1,0:T(8,128)(2,1)} %get-tuple-element.12) | copy-start | bytes 1152004
  161.4 11.4 %collective-permute-start.2 = (bf16[1,1,16,12000]{3,2,1,0:T(8,128)(2,1)}, bf16[1,1,16,12000]{3,2,1,0:T(8,128)(2,1)S(1)}, u32[]{:S(2)}, u32[]{:S(2)}) collective-permute-start(bf16[1,1,16,12000]{3,2,1,0:T(8,128)(2,1)} %get-tuple-element.20), channel_id=1, source_target_pairs={{0,3},{1,2},{2,1},{3,0},{4,7},{5,6},{6,5},{7,4},{8,11},{9,10},{10,... | collective-permute-start | bytes 1152008 | tf_op jit(solution)/shard_map/ppermute | solution.py:122
  172.8 11.1 %collective-permute-start.3 = (bf16[1,1,16,12000]{3,2,1,0:T(8,128)(2,1)}, bf16[1,1,16,12000]{3,2,1,0:T(8,128)(2,1)S(1)}, u32[]{:S(2)}, u32[]{:S(2)}) collective-permute-start(bf16[1,1,16,12000]{3,2,1,0:T(8,128)(2,1)} %get-tuple-element.19), channel_id=1, source_target_pairs={{0,4},{1,5},{2,6},{3,7},{4,0},{5,1},{6,2},{7,3},{8,12},{9,13},{10,... | collective-permute-start | bytes 1152008 | tf_op jit(solution)/shard_map/ppermute | solution.py:122
  183.9 10.8 %collective-permute-start.4 = (bf16[1,1,16,12000]{3,2,1,0:T(8,128)(2,1)}, bf16[1,1,16,12000]{3,2,1,0:T(8,128)(2,1)S(1)}, u32[]{:S(2)}, u32[]{:S(2)}) collective-permute-start(bf16[1,1,16,12000]{3,2,1,0:T(8,128)(2,1)} %get-tuple-element.18), channel_id=1, source_target_pairs={{0,5},{1,4},{2,7},{3,6},{4,1},{5,0},{6,3},{7,2},{8,13},{9,12},{10,... | collective-permute-start | bytes 1152008 | tf_op jit(solution)/shard_map/ppermute | solution.py:122
  194.7 11.2 %collective-permute-start.5 = (bf16[1,1,16,12000]{3,2,1,0:T(8,128)(2,1)S(1)}, bf16[1,1,16,12000]{3,2,1,0:T(8,128)(2,1)S(1)}, u32[]{:S(2)}, u32[]{:S(2)}) collective-permute-start(bf16[1,1,16,12000]{3,2,1,0:T(8,128)(2,1)S(1)} %copy-done.24), channel_id=1, source_target_pairs={{0,6},{1,7},{2,4},{3,5},{4,2},{5,3},{6,0},{7,1},{8,14},{9,15},{10,... | collective-permute-start | bytes 1152008 | tf_op jit(solution)/shard_map/ppermute | solution.py:122
  206.0 11.6 %collective-permute-start.6 = (bf16[1,1,16,12000]{3,2,1,0:T(8,128)(2,1)S(1)}, bf16[1,1,16,12000]{3,2,1,0:T(8,128)(2,1)S(1)}, u32[]{:S(2)}, u32[]{:S(2)}) collective-permute-start(bf16[1,1,16,12000]{3,2,1,0:T(8,128)(2,1)S(1)} %copy-done.23), channel_id=1, source_target_pairs={{0,7},{1,6},{2,5},{3,4},{4,3},{5,2},{6,1},{7,0},{8,15},{9,14},{10,... | collective-permute-start | bytes 1152008 | tf_op jit(solution)/shard_map/ppermute | solution.py:122
  217.6 20.2 %collective-permute-start.7 = (bf16[1,1,16,12000]{3,2,1,0:T(8,128)(2,1)S(1)}, bf16[1,1,16,12000]{3,2,1,0:T(8,128)(2,1)S(1)}, u32[]{:S(2)}, u32[]{:S(2)}) collective-permute-start(bf16[1,1,16,12000]{3,2,1,0:T(8,128)(2,1)S(1)} %copy-done.22), channel_id=1, source_target_pairs={{0,8},{1,9},{2,10},{3,11},{4,12},{5,13},{6,14},{7,15},{8,0},{9,1},... | collective-permute-start | bytes 1152008 | tf_op jit(solution)/shard_map/ppermute | solution.py:122
  237.7 20.0 %collective-permute-start.8 = (bf16[1,1,16,12000]{3,2,1,0:T(8,128)(2,1)S(1)}, bf16[1,1,16,12000]{3,2,1,0:T(8,128)(2,1)S(1)}, u32[]{:S(2)}, u32[]{:S(2)}) collective-permute-start(bf16[1,1,16,12000]{3,2,1,0:T(8,128)(2,1)S(1)} %copy-done.21), channel_id=1, source_target_pairs={{0,9},{1,8},{2,11},{3,10},{4,13},{5,12},{6,15},{7,14},{8,1},{9,0},... | collective-permute-start | bytes 1152008 | tf_op jit(solution)/shard_map/ppermute | solution.py:122
  257.7 19.2 %collective-permute-start.9 = (bf16[1,1,16,12000]{3,2,1,0:T(8,128)(2,1)S(1)}, bf16[1,1,16,12000]{3,2,1,0:T(8,128)(2,1)S(1)}, u32[]{:S(2)}, u32[]{:S(2)}) collective-permute-start(bf16[1,1,16,12000]{3,2,1,0:T(8,128)(2,1)S(1)} %copy-done.20), channel_id=1, source_target_pairs={{0,10},{1,11},{2,8},{3,9},{4,14},{5,15},{6,12},{7,13},{8,2},{9,3},... | collective-permute-start | bytes 1152008 | tf_op jit(solution)/shard_map/ppermute | solution.py:122
  276.9 20.4 %collective-permute-start.10 = (bf16[1,1,16,12000]{3,2,1,0:T(8,128)(2,1)S(1)}, bf16[1,1,16,12000]{3,2,1,0:T(8,128)(2,1)S(1)}, u32[]{:S(2)}, u32[]{:S(2)}) collective-permute-start(bf16[1,1,16,12000]{3,2,1,0:T(8,128)(2,1)S(1)} %copy-done.19), channel_id=1, source_target_pairs={{0,11},{1,10},{2,9},{3,8},{4,15},{5,14},{6,13},{7,12},{8,3},{9,2},... | collective-permute-start | bytes 1152008 | tf_op jit(solution)/shard_map/ppermute | solution.py:122
  304.7 1.4 copy-start.17
  304.7 1.9 copy-start.18
  306.6 1.4 copy-start.15
  306.6 1.9 copy-start.16
  308.4 1.4 copy-start.13
  308.4 1.9 copy-start.14
  310.3 1.4 copy-start.11
  310.3 1.9 copy-start.12
  312.2 1.4 copy-start.9
  312.2 1.9 copy-start.10
  314.0 1.4 copy-start.7
  314.0 1.9 copy-start.8
  315.9 1.4 copy-start.5
  315.9 1.9 copy-start.6
  317.7 1.4 copy-start.3
  317.8 1.9 copy-start.4
  394.7 3.5 copy-start.1
Sparse Core Ops, SparseCore 0:
  322.8 48.7 all-gather.1
